TPU v7x, 32 devices: a whole 2x2x4 slice. The times are simulated.
32 devices in a mesh: ctx: 2 (over x), req: 4 (over y, core), mp: 4 (over z).
Axes of the slice: x: 2, y: 2, z: 4, core: 2. Of those that a mesh axis runs over, the one named last changes fastest.
Arguments:
- activations: bfloat16 [4, 256, 8192], P('req', 'ctx', 'mp'), may hold values from -6 to 6
- query_base: bfloat16 [4, 256, 8192], P('req', 'ctx', 'mp'), may hold values from -9 to 9
- key_base: bfloat16 [4, 256, 1024], P('req', 'ctx', 'mp'), may hold values from -9 to 9
- plain_value_rows: bfloat16 [4, 256, 1024], P('req', 'ctx', 'mp'), may hold values from -6 to 6
- query_down: bfloat16 [8, 64, 8192], P('req', 'ctx', 'mp'), may hold values from -0.0625 to 0.0625
- query_up: bfloat16 [8, 64, 8192], P('req', 'ctx', 'mp'), may hold values from -0.75 to 0.75
- value_down: bfloat16 [8, 64, 8192], P('req', 'ctx', 'mp'), may hold values from -0.0625 to 0.0625
- value_raise_factor: bfloat16 [8, 64, 1024], P('req', 'ctx', 'mp'), may hold values from -0.75 to 0.75
- member_lists: int32 [4, 2], P('req'), may hold values from 0 to 7
- prompt_lengths: int32 [4], P('req'), may hold values from 32 to 256, as said below
Outputs:
- attended: bfloat16 [2, 4, 256, 8192], P(None, 'req', 'ctx', 'mp')
Inputs may be any that keep to these rules, and one draw needn't show every extreme that they name: `prompt_lengths`: at least one prompt has all 256 positions live.
All inputs are finite; a program needn't handle non-finite values.
Results may differ from a plain program's by a relative error of at most 0.008.
Values may be sent and summed in bfloat16 or wider, within the bound.
No kernel may reach another device: no remote copies, remote signals or barrier semaphores. Data moves between devices by JAX's collectives and lax.ppermute only.
A program may use at most 64 MiB of HBM per device.

v0:
```python
import math
import jax
import jax.numpy as jnp
from jax import lax
from jax.sharding import PartitionSpec as P

HEAD_SIZE = 128


def block_rows(total_rows):
    if total_rows <= 512:
        return total_rows
    for candidate in range(512, 0, -1):
        if total_rows % candidate == 0:
            return candidate
    return total_rows


def select_members(factor_set, member_ids, member_count):
    onehot = (member_ids[:, None] == jnp.arange(member_count, dtype=jnp.int32)[None, :]).astype(
        jnp.bfloat16
    )
    return tuple(
        (
            jnp.einsum("sm,mkc->skc", onehot, factor, preferred_element_type=jnp.float32).astype(
                jnp.bfloat16
            )
            for factor in factor_set
        )
    )


def per_device(
    activations,
    query_base,
    key_base,
    plain_value_rows,
    query_down,
    query_up,
    value_down,
    value_raise_factor,
    member_lists,
    prompt_lengths,
):
    row_count = activations.shape[1]
    member_count = query_down.shape[0] * lax.axis_size("req")
    member_ids = member_lists[0]
    full_rank = (
        lax.all_gather(query_down, "ctx", axis=1, tiled=True),
        lax.all_gather(query_up, "ctx", axis=1, tiled=True),
        lax.all_gather(value_down, "ctx", axis=1, tiled=True),
        lax.all_gather(value_raise_factor, "ctx", axis=1, tiled=True),
    )
    all_members = (
        lax.all_gather(full_rank[0], "req", axis=0, tiled=True),
        lax.all_gather(full_rank[1], "req", axis=0, tiled=True),
        lax.all_gather(full_rank[2], "req", axis=0, tiled=True),
        lax.all_gather(full_rank[3], "req", axis=0, tiled=True),
    )
    chosen = select_members(all_members, member_ids, member_count)
    down_query, up_query, down_value, up_value = chosen
    tokens = activations[0]
    rank_query = jnp.einsum("rd,skd->rsk", tokens, down_query, preferred_element_type=jnp.float32)
    rank_value = jnp.einsum("rd,skd->rsk", tokens, down_value, preferred_element_type=jnp.float32)
    rank_query, rank_value = lax.psum((rank_query, rank_value), "mp")
    rank_query = rank_query.astype(jnp.bfloat16)
    rank_value = rank_value.astype(jnp.bfloat16)
    query_matrix = (
        query_base[0][:, None, :]
        + jnp.einsum("rsk,skc->rsc", rank_query, up_query, preferred_element_type=jnp.float32)
    ).astype(jnp.bfloat16)
    slot_count = query_matrix.shape[1]
    rank_width = rank_value.shape[2]
    group_count = key_base.shape[2] // HEAD_SIZE
    group_portion = query_matrix.shape[2] // (group_count * HEAD_SIZE)
    grouped = query_matrix.reshape(row_count, slot_count, group_count, group_portion, HEAD_SIZE)
    rows_of_keys = key_base[0]
    positions = lax.axis_index("ctx") * row_count + jnp.arange(row_count, dtype=jnp.int32)
    live_length = prompt_lengths[0]
    inverse = 1.0 / math.sqrt(HEAD_SIZE)

    def update(running, key_block, value_block, key_start):
        run_max, run_total, accumulated = running
        block_length = key_block.shape[0]
        heads_of_keys = key_block.reshape(block_length, group_count, HEAD_SIZE)
        heads_of_values = value_block.reshape(block_length, slot_count, group_count, HEAD_SIZE)
        scores = (
            jnp.einsum(
                "rsgjd,kgd->sgjrk", grouped, heads_of_keys, preferred_element_type=jnp.float32
            )
            * inverse
        )
        key_positions = key_start + jnp.arange(block_length, dtype=jnp.int32)
        visible = (key_positions[None, :] <= positions[:, None]) & (
            key_positions[None, :] < live_length
        )
        masked = jnp.where(visible, scores, -1e30)
        new_max = jnp.maximum(run_max, jnp.max(masked, axis=-1))
        weights = jnp.where(visible, jnp.exp(masked - new_max[..., None]), 0.0)
        factor = jnp.exp(run_max - new_max)
        new_total = run_total * factor + jnp.sum(weights, axis=-1)
        new_accumulated = accumulated * factor[..., None] + jnp.einsum(
            "sgjrk,ksgd->sgjrd",
            weights.astype(jnp.bfloat16),
            heads_of_values,
            preferred_element_type=jnp.float32,
        )
        return (new_max, new_total, new_accumulated)

    initial = (
        jnp.full((slot_count, group_count, group_portion, row_count), -1e30, jnp.float32),
        jnp.zeros((slot_count, group_count, group_portion, row_count), jnp.float32),
        jnp.zeros((slot_count, group_count, group_portion, row_count, HEAD_SIZE), jnp.float32),
    )
    base_rows = plain_value_rows[0]
    piece_rows = base_rows.shape[0]
    ranks = rank_value.reshape(row_count, slot_count * rank_width).reshape(
        piece_rows, slot_count, rank_width
    )
    built = (
        base_rows[:, None, :]
        + jnp.einsum("rsk,skc->rsc", ranks, up_value, preferred_element_type=jnp.float32)
    ).astype(jnp.bfloat16)
    packed = built.reshape(piece_rows, slot_count * group_count * HEAD_SIZE)
    key_piece = lax.all_gather(rows_of_keys, "ctx", axis=0, tiled=True)
    value_piece = lax.all_gather(packed, "ctx", axis=0, tiled=True)
    first_row = jnp.int32(0)
    piece_rows = key_piece.shape[0]
    step_rows = block_rows(piece_rows)

    def advance(block_index, current):
        offset = block_index * step_rows
        key_block = lax.dynamic_slice_in_dim(key_piece, offset, step_rows, 0)
        value_block = lax.dynamic_slice_in_dim(value_piece, offset, step_rows, 0)
        key_start = first_row + offset
        return update(current, key_block, value_block, key_start)

    run_max, run_total, accumulated = lax.fori_loop(0, piece_rows // step_rows, advance, initial)
    result = accumulated / run_total[..., None]
    result = (
        jnp.transpose(result, (0, 3, 1, 2, 4))
        .reshape(slot_count, row_count, group_count * group_portion * HEAD_SIZE)
        .astype(jnp.bfloat16)
    )
    return result[:, None]


def solution(mesh):
    in_specs = (
        P("req", "ctx", "mp"),
        P("req", "ctx", "mp"),
        P("req", "ctx", "mp"),
        P("req", "ctx", "mp"),
        P("req", "ctx", "mp"),
        P("req", "ctx", "mp"),
        P("req", "ctx", "mp"),
        P("req", "ctx", "mp"),
        P("req", None),
        P("req"),
    )
    out_specs = P(None, "req", "ctx", "mp")
    return jax.shard_map(
        per_device, mesh=mesh, in_specs=in_specs, out_specs=out_specs, check_vma=False
    )
```

profile of v0, /device:TPU:0, one launch (start us, length us, event | category | flops | bytes accessed | tf_op | source)
XLA Modules:
  0.0 111.7 jit_solution(13145723315272196515)
XLA Ops:
  6.5 12.0 %all_gather.37 = bf16[2,64,2048]{2,1,0:T(8,128)(2,1)} all-gather(bf16[2,32,2048]{2,1,0:T(8,128)(2,1)} %param.16), channel_id=1, replica_groups=mesh['ctx'=2,'req'=4,'mp'=4] {'ctx'}, dimensions={1}, use_global_device_ids=true | all-gather | bytes 786432 | tf_op jit(solution)/shard_map/all_gather | solution.py:51
  18.6 8.5 %all_gather.32 = bf16[2,64,2048]{2,1,0:T(8,128)(2,1)} all-gather(bf16[2,32,2048]{2,1,0:T(8,128)(2,1)} %param.14), channel_id=1, replica_groups=mesh['ctx'=2,'req'=4,'mp'=4] {'ctx'}, dimensions={1}, use_global_device_ids=true | all-gather | bytes 786432 | tf_op jit(solution)/shard_map/all_gather | solution.py:49
  27.2 7.9 %all_gather.30 = bf16[2,64,2048]{2,1,0:T(8,128)(2,1)} all-gather(bf16[2,32,2048]{2,1,0:T(8,128)(2,1)S(1)} %copy-done.2), channel_id=1, replica_groups=mesh['ctx'=2,'req'=4,'mp'=4] {'ctx'}, dimensions={1}, use_global_device_ids=true | all-gather | bytes 786432 | tf_op jit(solution)/shard_map/all_gather | solution.py:50
  35.1 0.1 bitcast_convert_fusion
  35.2 0.3 copy.27
  36.2 0.1 copy.32
  36.5 4.6 %all_gather.35 = bf16[2,64,256]{2,1,0:T(8,128)(2,1)S(1)} all-gather(bf16[2,32,256]{2,1,0:T(8,128)(2,1)S(1)} %copy-done.5), channel_id=1, replica_groups=mesh['ctx'=2,'req'=4,'mp'=4] {'ctx'}, dimensions={1}, use_global_device_ids=true | all-gather | bytes 98304 | tf_op jit(solution)/shard_map/all_gather | solution.py:52
  41.0 5.0 %all-gather = bf16[1,256,256]{1,2,0:T(8,128)(2,1)S(1)} all-gather(bf16[1,128,256]{1,2,0:T(8,128)(2,1)S(1)} %copy.32), channel_id=2, replica_groups=mesh['ctx'=2,'req'=4,'mp'=4] {'ctx'}, dimensions={1}, use_global_device_ids=true | all-gather | bytes 196608 | tf_op jit(solution)/shard_map/all_gather | solution.py:125
  46.0 6.0 %all_gather.36 = bf16[8,64,256]{2,1,0:T(8,128)(2,1)S(1)} all-gather(bf16[2,64,256]{2,1,0:T(8,128)(2,1)S(1)} %all_gather.35), channel_id=1, replica_groups=mesh['ctx'=2,'req'=4,'mp'=4] {'req'}, dimensions={0}, use_global_device_ids=true | all-gather | bytes 327680 | tf_op jit(solution)/shard_map/all_gather | solution.py:58
  52.1 0.3 convolution_convert_fusion.3
  52.5 3.1 %convolution_convert_fusion = bf16[2,64,2048]{2,0,1:T(2,128)(2,1)S(1)} fusion(bf16[8,64,2048]{2,1,0:T(8,128)(2,1)} %all-gather.9.cloned.1.call-done, s32[2]{0:T(128)S(1)} %bitcast.86), kind=kOutput, calls=%fused_computation.10 | convolution fusion | flops 4456464 | bytes 2621448 | tf_op jit(solution)/shard_map/sm,mkc->skc/dot_general | solution.py:25
  55.6 0.4 convolution_bitcast_fusion.2
  56.0 9.8 %all-gather.7.cloned.1.call-done = bf16[8,64,2048]{2,1,0:T(8,128)(2,1)} async-done(((bf16[2,64,2048]{2,1,0:T(8,128)(2,1)}), bf16[8,64,2048]{2,1,0:T(8,128)(2,1)}) %all-gather.7.cloned.1.call-update) | async-done | bytes 2097168 | tf_op jit(solution)/shard_map/all_gather | solution.py:55
  65.8 3.1 %convolution_convert_fusion.1 = bf16[2,64,2048]{2,0,1:T(2,128)(2,1)S(1)} fusion(bf16[8,64,2048]{2,1,0:T(8,128)(2,1)} %all-gather.7.cloned.1.call-done, s32[2]{0:T(128)S(1)} %bitcast.87), kind=kOutput, calls=%fused_computation.11 | convolution fusion | flops 4456464 | bytes 2621448 | tf_op jit(solution)/shard_map/sm,mkc->skc/dot_general | solution.py:25
  68.9 0.4 convolution_bitcast_fusion.3
  69.3 21.2 %all-reduce.2 = (bf16[128,2,64]{0,2,1:T(8,128)(2,1)S(1)}, bf16[128,2,64]{0,2,1:T(8,128)(2,1)S(1)}) all-reduce(f32[128,2,64]{0,2,1:T(8,128)S(1)} %convolution_bitcast_fusion.2, f32[128,2,64]{0,2,1:T(8,128)S(1)} %convolution_bitcast_fusion.3), channel_id=1, replica_groups=mesh['ctx'=2,'req'=4,'mp'=4] {'mp'}, use_global_device_ids=true, to_apply=%region_2.3 | all-reduce | flops 32768 | bytes 196608 | tf_op jit(solution)/shard_map/psum | solution.py:65
  90.5 3.1 %convolution_convert_fusion.2 = bf16[2,64,2048]{2,0,1:T(2,128)(2,1)S(1)} fusion(bf16[8,64,2048]{2,1,0:T(8,128)(2,1)} %all-gather.5.cloned.1.call-done, s32[2]{0:T(128)S(1)} %bitcast.88), kind=kOutput, calls=%fused_computation.12 | convolution fusion | flops 4456464 | bytes 2621448 | tf_op jit(solution)/shard_map/sm,mkc->skc/dot_general | solution.py:25
  93.7 0.6 fusion.5
  94.2 1.0 bitcast_reduce_fusion
  95.3 1.7 %fusion.2 = (f32[2,2,8,128]{3,2,0,1:T(8,128)S(1)}, bf16[2,2,8,128,256]{4,3,2,0,1:T(8,128)(2,1)S(1)}) fusion(f32[2,128,2,8,256]{4,1,3,2,0:T(8,128)S(1)} %get-tuple-element.40, f32[2,2,8,128]{3,2,0,1:T(8,128)S(1)} %get-tuple-element.28, pred[128,256]{1,0:T(8,128)(4,1)S(1)} %fusion.25), kind=kLoop, calls=%fused_computation.5 | loop fusion | flops 6287360 | bytes 6356992 | tf_op jit(solution)/shard_map/while/body/eval_jaxpr/reduce_sum | solution.py:101
  97.0 0.2 fusion.16
  97.3 5.8 %all_gather.39 = bf16[256,512]{0,1:T(8,128)(2,1)S(1)} all-gather(bf16[128,512]{0,1:T(8,128)(2,1)S(1)} %bitcast.83), channel_id=1, replica_groups=mesh['ctx'=2,'req'=4,'mp'=4] {'ctx'}, dimensions={0}, use_global_device_ids=true | all-gather | bytes 393216 | tf_op jit(solution)/shard_map/all_gather | solution.py:126
  103.1 0.8 fusion.7
  103.9 1.3 %copy.43 = bf16[2,1,128,2048]{3,2,1,0:T(8,128)(2,1)} copy(bf16[2,1,128,2048]{2,3,0,1:T(8,128)(2,1)S(1)} %bitcast.81) | data formatting | bytes 2097152 | tf_op jit(solution)/shard_map/convert_element_type | solution.py:143
  (29 shorter events, 0.4 us)
Async XLA Ops:
  6.5 49.1 %copy-start = (bf16[1,128,2048]{2,1,0:T(8,128)(2,1)S(1)}, bf16[1,128,2048]{2,1,0:T(8,128)(2,1)}, u32[]{:S(2)}) copy-start(bf16[1,128,2048]{2,1,0:T(8,128)(2,1)} %param.10) | copy-start | bytes 1572868
  6.5 20.6 %copy-start.2 = (bf16[2,32,2048]{2,1,0:T(8,128)(2,1)S(1)}, bf16[2,32,2048]{2,1,0:T(8,128)(2,1)}, u32[]{:S(2)}) copy-start(bf16[2,32,2048]{2,1,0:T(8,128)(2,1)} %param.15) | copy-start | bytes 786436
  6.5 28.5 %copy-start.1 = (bf16[1,128,2048]{2,1,0:T(8,128)(2,1)S(1)}, bf16[1,128,2048]{2,1,0:T(8,128)(2,1)}, u32[]{:S(2)}) copy-start(bf16[1,128,2048]{2,1,0:T(8,128)(2,1)} %param.11) | copy-start | bytes 1572868
  6.5 45.9 %all-gather.9.cloned.1.call-start = ((), (), s32[]{:S(2)}) async-start(), calls=%async_computation.2 | async-start | bytes 2621440 | tf_op jit(solution)/shard_map/all_gather | solution.py:57
  18.6 47.2 %all-gather.7.cloned.1.call-start = ((), (), s32[]{:S(2)}) async-start(), calls=%async_computation.1 | async-start | bytes 2621440 | tf_op jit(solution)/shard_map/all_gather | solution.py:55
  27.1 63.4 %all-gather.5.cloned.1.call-start = ((), (), s32[]{:S(2)}) async-start(), calls=%async_computation | async-start | bytes 2621440 | tf_op jit(solution)/shard_map/all_gather | solution.py:56
  35.0 1.2 %copy-start.4 = (bf16[1,128,256]{2,1,0:T(8,128)(2,1)S(1)}, bf16[1,128,256]{2,1,0:T(8,128)(2,1)}, u32[]{:S(2)}) copy-start(bf16[1,128,256]{2,1,0:T(8,128)(2,1)} %param.12) | copy-start | bytes 196612
  35.0 1.3 %copy-start.3 = (bf16[1,128,256]{2,1,0:T(8,128)(2,1)S(1)}, bf16[1,128,256]{2,1,0:T(8,128)(2,1)}, u32[]{:S(2)}) copy-start(bf16[1,128,256]{2,1,0:T(8,128)(2,1)} %param.13) | copy-start | bytes 196612
  35.1 1.4 %copy-start.5 = (bf16[2,32,256]{2,1,0:T(8,128)(2,1)S(1)}, bf16[2,32,256]{2,1,0:T(8,128)(2,1)}, u32[]{:S(2)}) copy-start(bf16[2,32,256]{2,1,0:T(8,128)(2,1)} %param.17) | copy-start | bytes 98308
  35.1 17.0 %copy-start.6 = (s32[1,2]{1,0:T(1,128)S(1)}, s32[1,2]{1,0:T(1,128)}, u32[]{:S(2)}) copy-start(s32[1,2]{1,0:T(1,128)} %param.18) | copy-start | bytes 28
Sparse Core Ops, SparseCore 0:
  18.7 22.8 all-gather.8
  43.2 22.5 all-gather.6
  67.4 22.5 all-gather.4
where the time goes:
time: 112 us
  blocking collectives  70.8 us (63%)
  between operations  14 us (12%)
  matrix products  13.1 us (12%)
  waiting for transfers between devices  9.9 us (9%)
  other arithmetic  1.96 us (2%)
  local copies, waits for them, and re-layouts  1.87 us (2%)
    psum x1, blocking collectives, per_device(): rank_query, rank_value = lax.psum((rank_query, rank_value), 'mp')  21.2 us
    all_gather x1, blocking collectives, per_device(): lax.all_gather(value_down, 'ctx', axis=1, tiled=True)  12 us
    all_gather x1, waiting for transfers between devices, per_device(): lax.all_gather(full_rank[0], 'req', axis=0, tiled=True)  9.81 us
    dot_general x4, matrix products, select_members(): jnp.einsum('sm,mkc->skc', onehot, factor, preferred_element_type=jnp.floa...  9.69 us
    all_gather x1, blocking collectives, per_device(): lax.all_gather(query_down, 'ctx', axis=1, tiled=True)  8.45 us
    all_gather x1, blocking collectives, per_device(): lax.all_gather(query_up, 'ctx', axis=1, tiled=True)  7.85 us
    all_gather x1, blocking collectives, per_device(): lax.all_gather(full_rank[3], 'req', axis=0, tiled=True)  6.01 us
    all_gather x1, blocking collectives, per_device(): value_piece = lax.all_gather(packed, 'ctx', axis=0, tiled=True)  5.77 us
  transfers between devices with their start and end apart: 3, of which 1 were waited for; matrix products, arithmetic and copies ran while one was open for 7% of the time, Pallas kernels for 0%

commit v1 on v0

--- a/solution.py
+++ b/solution.py
@@ -122,8 +122,17 @@
         + jnp.einsum("rsk,skc->rsc", ranks, up_value, preferred_element_type=jnp.float32)
     ).astype(jnp.bfloat16)
     packed = built.reshape(piece_rows, slot_count * group_count * HEAD_SIZE)
-    key_piece = lax.all_gather(rows_of_keys, "ctx", axis=0, tiled=True)
-    value_piece = lax.all_gather(packed, "ctx", axis=0, tiled=True)
+
+    def change_the_ratios(array_in, packet):
+        return jnp.split(
+            lax.all_gather(
+                jnp.concatenate([array_in, packet], axis=1), tiled=True, axis=0, axis_name="ctx"
+            ),
+            [array_in.shape[1]],
+            axis=1,
+        )
+
+    key_piece, value_piece = change_the_ratios(rows_of_keys, packed)
     first_row = jnp.int32(0)
     piece_rows = key_piece.shape[0]
     step_rows = block_rows(piece_rows)

time: 112 us -> 112 us (level)
  waiting for transfers between devices: 9.9 us -> 14.6 us
  blocking collectives: 70.8 us -> 66.5 us
    all_gather x1, waiting for transfers between devices: 0.02 us -> 14.5 us  [per_device(): lax.all_gather(full_rank[2], 'req', axis=0, tiled=True)]
    all_gather x1, waiting for transfers between devices: 9.81 us -> 0.02 us  [per_device(): lax.all_gather(full_rank[0], 'req', axis=0, tiled=True)]
    all_gather x2 -> x1, blocking collectives: 10.7 us -> 6.37 us  [change_the_ratios(): lax.all_gather(jnp.concatenate([array_in, packet], axis=1), tiled=True, a...]
    all_gather x1, blocking collectives: 12 us -> 8.45 us  [per_device(): lax.all_gather(value_down, 'ctx', axis=1, tiled=True)]
    all_gather x1, blocking collectives: 8.45 us -> 12 us  [per_device(): lax.all_gather(query_down, 'ctx', axis=1, tiled=True)]
where the time goes in v1:
time: 112 us
  blocking collectives  66.5 us (59%)
  waiting for transfers between devices  14.6 us (13%)
  between operations  14 us (12%)
  matrix products  12.7 us (11%)
  local copies, waits for them, and re-layouts  2.05 us (2%)
  other arithmetic  1.54 us (1%)
    psum x1, blocking collectives, per_device(): rank_query, rank_value = lax.psum((rank_query, rank_value), 'mp')  21.2 us
    all_gather x1, waiting for transfers between devices, per_device(): lax.all_gather(full_rank[2], 'req', axis=0, tiled=True)  14.5 us
    all_gather x1, blocking collectives, per_device(): lax.all_gather(query_down, 'ctx', axis=1, tiled=True)  12 us
    dot_general x4, matrix products, select_members(): jnp.einsum('sm,mkc->skc', onehot, factor, preferred_element_type=jnp.floa...  9.86 us
    all_gather x1, blocking collectives, per_device(): lax.all_gather(value_down, 'ctx', axis=1, tiled=True)  8.45 us
    all_gather x1, blocking collectives, per_device(): lax.all_gather(query_up, 'ctx', axis=1, tiled=True)  7.85 us
    all_gather x1, blocking collectives, change_the_ratios(): lax.all_gather(jnp.concatenate([array_in, packet], axis=1), tiled=True, a...  6.37 us
    all_gather x1, blocking collectives, per_device(): lax.all_gather(full_rank[3], 'req', axis=0, tiled=True)  6.03 us
  transfers between devices with their start and end apart: 3, of which 1 were waited for; matrix products, arithmetic and copies ran while one was open for 7% of the time, Pallas kernels for 0%

profile of v1, /device:TPU:0, one launch (start us, length us, event | category | flops | bytes accessed | tf_op | source)
XLA Modules:
  0.0 111.5 jit_solution(11985317121509348231)
XLA Ops:
  6.6 12.0 %all_gather.34 = bf16[2,64,2048]{2,1,0:T(8,128)(2,1)} all-gather(bf16[2,32,2048]{2,1,0:T(8,128)(2,1)} %param.14), channel_id=1, replica_groups=mesh['ctx'=2,'req'=4,'mp'=4] {'ctx'}, dimensions={1}, use_global_device_ids=true | all-gather | bytes 786432 | tf_op jit(solution)/shard_map/all_gather | solution.py:49
  18.7 8.5 %all_gather.29 = bf16[2,64,2048]{2,1,0:T(8,128)(2,1)} all-gather(bf16[2,32,2048]{2,1,0:T(8,128)(2,1)} %param.16), channel_id=1, replica_groups=mesh['ctx'=2,'req'=4,'mp'=4] {'ctx'}, dimensions={1}, use_global_device_ids=true | all-gather | bytes 786432 | tf_op jit(solution)/shard_map/all_gather | solution.py:51
  27.2 7.9 %all_gather.32 = bf16[2,64,2048]{2,1,0:T(8,128)(2,1)} all-gather(bf16[2,32,2048]{2,1,0:T(8,128)(2,1)S(1)} %copy-done.3), channel_id=1, replica_groups=mesh['ctx'=2,'req'=4,'mp'=4] {'ctx'}, dimensions={1}, use_global_device_ids=true | all-gather | bytes 786432 | tf_op jit(solution)/shard_map/all_gather | solution.py:50
  35.8 0.1 copy.28
  36.2 0.3 copy.34
  36.5 0.2 copy-done.6
  36.7 4.6 %all_gather.27 = bf16[2,64,256]{2,1,0:T(8,128)(2,1)S(1)} all-gather(bf16[2,32,256]{2,1,0:T(8,128)(2,1)S(1)} %copy-done.6), channel_id=1, replica_groups=mesh['ctx'=2,'req'=4,'mp'=4] {'ctx'}, dimensions={1}, use_global_device_ids=true | all-gather | bytes 98304 | tf_op jit(solution)/shard_map/all_gather | solution.py:52
  41.2 6.0 %all_gather.28 = bf16[8,64,256]{2,1,0:T(8,128)(2,1)S(1)} all-gather(bf16[2,64,256]{2,1,0:T(8,128)(2,1)S(1)} %all_gather.27), channel_id=1, replica_groups=mesh['ctx'=2,'req'=4,'mp'=4] {'req'}, dimensions={0}, use_global_device_ids=true | all-gather | bytes 327680 | tf_op jit(solution)/shard_map/all_gather | solution.py:58
  47.3 0.1 fusion.24
  47.4 0.3 convolution_convert_fusion.3
  47.7 3.2 %convolution_convert_fusion = bf16[2,64,2048]{2,0,1:T(2,128)(2,1)S(1)} fusion(bf16[8,64,2048]{2,1,0:T(8,128)(2,1)} %all-gather.8.cloned.1.call-done, s32[2]{0:T(128)S(1)} %bitcast.87), kind=kOutput, calls=%fused_computation.8 | convolution fusion | flops 4456464 | bytes 2621448 | tf_op jit(solution)/shard_map/sm,mkc->skc/dot_general | solution.py:25
  50.9 0.4 convolution_bitcast_fusion.2
  51.3 14.5 %all-gather.4.cloned.1.call-done = bf16[8,64,2048]{2,1,0:T(8,128)(2,1)} async-done(((bf16[2,64,2048]{2,1,0:T(8,128)(2,1)}), bf16[8,64,2048]{2,1,0:T(8,128)(2,1)}) %all-gather.4.cloned.1.call-update) | async-done | bytes 2097168 | tf_op jit(solution)/shard_map/all_gather | solution.py:57
  65.8 3.1 %convolution_convert_fusion.2 = bf16[2,64,2048]{2,0,1:T(2,128)(2,1)S(1)} fusion(bf16[8,64,2048]{2,1,0:T(8,128)(2,1)} %all-gather.4.cloned.1.call-done, s32[2]{0:T(128)S(1)} %bitcast.88), kind=kOutput, calls=%fused_computation.10 | convolution fusion | flops 4456464 | bytes 2621448 | tf_op jit(solution)/shard_map/sm,mkc->skc/dot_general | solution.py:25
  69.0 0.4 convolution_bitcast_fusion.3
  69.4 21.2 %all-reduce.2 = (bf16[128,2,64]{0,2,1:T(8,128)(2,1)S(1)}, bf16[128,2,64]{0,2,1:T(8,128)(2,1)S(1)}) all-reduce(f32[128,2,64]{0,2,1:T(8,128)S(1)} %convolution_bitcast_fusion.3, f32[128,2,64]{0,2,1:T(8,128)S(1)} %convolution_bitcast_fusion.2), channel_id=1, replica_groups=mesh['ctx'=2,'req'=4,'mp'=4] {'mp'}, use_global_device_ids=true, to_apply=%region_0.0 | all-reduce | flops 32768 | bytes 196608 | tf_op jit(solution)/shard_map/psum | solution.py:65
  90.5 0.2 fusion.15
  90.8 6.4 %all_gather.31 = bf16[256,768]{0,1:T(8,128)(2,1)S(1)} all-gather(bf16[128,768]{0,1:T(8,128)(2,1)S(1)} %pad_maximum_fusion), channel_id=1, replica_groups=mesh['ctx'=2,'req'=4,'mp'=4] {'ctx'}, dimensions={0}, use_global_device_ids=true | all-gather | bytes 589824 | tf_op jit(solution)/shard_map/all_gather | solution.py:128
  97.2 3.2 %convolution_convert_fusion.1 = bf16[2,64,2048]{2,0,1:T(2,128)(2,1)S(1)} fusion(bf16[8,64,2048]{2,1,0:T(8,128)(2,1)} %all-gather.6.cloned.1.call-done, s32[2]{0:T(128)S(1)} %bitcast.89), kind=kOutput, calls=%fused_computation.9 | convolution fusion | flops 4456464 | bytes 2621448 | tf_op jit(solution)/shard_map/sm,mkc->skc/dot_general | solution.py:25
  100.5 0.6 fusion.4
  101.1 0.8 fusion
  101.9 1.3 %fusion.1 = (f32[2,2,8,128]{3,2,0,1:T(8,128)S(1)}, bf16[2,2,8,128,256]{3,4,2,0,1:T(8,128)(2,1)S(1)}) fusion(f32[2,256,128,2,8]{2,1,4,3,0:T(8,128)S(1)} %get-tuple-element.40, f32[2,2,8,128]{3,2,0,1:T(8,128)S(1)} %get-tuple-element.28, pred[128,256]{0,1:T(8,128)(4,1)S(1)} %fusion.24), kind=kLoop, calls=%fused_computation.3 | loop fusion | flops 6287360 | bytes 6356992 | tf_op jit(solution)/shard_map/while/body/eval_jaxpr/reduce_sum | solution.py:101
  103.2 0.5 fusion.6
  103.7 1.3 %copy.44 = bf16[2,1,128,2048]{3,2,1,0:T(8,128)(2,1)} copy(bf16[2,1,128,2048]{2,3,0,1:T(8,128)(2,1)S(1)} %bitcast.82) | data formatting | bytes 2097152 | tf_op jit(solution)/shard_map/convert_element_type | solution.py:152
  (34 shorter events, 0.5 us)
Async XLA Ops:
  6.5 44.4 %copy-start = (bf16[1,128,2048]{2,1,0:T(8,128)(2,1)S(1)}, bf16[1,128,2048]{2,1,0:T(8,128)(2,1)}, u32[]{:S(2)}) copy-start(bf16[1,128,2048]{2,1,0:T(8,128)(2,1)} %param.10) | copy-start | bytes 1572868
  6.5 20.7 %copy-start.3 = (bf16[2,32,2048]{2,1,0:T(8,128)(2,1)S(1)}, bf16[2,32,2048]{2,1,0:T(8,128)(2,1)}, u32[]{:S(2)}) copy-start(bf16[2,32,2048]{2,1,0:T(8,128)(2,1)} %param.15) | copy-start | bytes 786436
  6.5 29.2 %copy-start.5 = (bf16[1,128,256]{2,1,0:T(8,128)(2,1)S(1)}, bf16[1,128,256]{2,1,0:T(8,128)(2,1)}, u32[]{:S(2)}) copy-start(bf16[1,128,256]{2,1,0:T(8,128)(2,1)} %param.12) | copy-start | bytes 196612
  6.5 29.3 %copy-start.4 = (bf16[1,128,256]{2,1,0:T(8,128)(2,1)S(1)}, bf16[1,128,256]{2,1,0:T(8,128)(2,1)}, u32[]{:S(2)}) copy-start(bf16[1,128,256]{2,1,0:T(8,128)(2,1)} %param.13) | copy-start | bytes 196612
  6.5 29.5 %copy-start.2 = (bf16[1,128,2048]{2,1,0:T(8,128)(2,1)S(1)}, bf16[1,128,2048]{2,1,0:T(8,128)(2,1)}, u32[]{:S(2)}) copy-start(bf16[1,128,2048]{2,1,0:T(8,128)(2,1)} %param.11) | copy-start | bytes 1572868
  6.5 41.2 %all-gather.8.cloned.1.call-start = ((), (), s32[]{:S(2)}) async-start(), calls=%async_computation.2 | async-start | bytes 2621440 | tf_op jit(solution)/shard_map/all_gather | solution.py:55
  18.6 47.2 %all-gather.4.cloned.1.call-start = ((), (), s32[]{:S(2)}) async-start(), calls=%async_computation | async-start | bytes 2621440 | tf_op jit(solution)/shard_map/all_gather | solution.py:57
  27.2 70.1 %all-gather.6.cloned.1.call-start = ((), (), s32[]{:S(2)}) async-start(), calls=%async_computation.1 | async-start | bytes 2621440 | tf_op jit(solution)/shard_map/all_gather | solution.py:56
  35.9 0.8 copy-start.6
  36.0 11.3 %copy-start.7 = (s32[1,2]{1,0:T(1,128)S(1)}, s32[1,2]{1,0:T(1,128)}, u32[]{:S(2)}) copy-start(s32[1,2]{1,0:T(1,128)} %param.18) | copy-start | bytes 28
  97.2 3.9 %copy-start.1 = (bf16[256,768]{0,1:T(8,128)(2,1)}, bf16[256,768]{0,1:T(8,128)(2,1)S(1)}, u32[]{:S(2)}) copy-start(bf16[256,768]{0,1:T(8,128)(2,1)S(1)} %all_gather.31) | copy-start | bytes 1179652
  101.9 1.3 %slice-start = ((bf16[256,768]{0,1:T(8,128)(2,1)}), bf16[256,512]{0,1:T(8,128)(2,1)S(1)}, s32[]{:S(2)}) async-start(bf16[256,768]{0,1:T(8,128)(2,1)} %copy-done.1), calls=%async_computation.3 | async-start | bytes 524288 | tf_op jit(solution)/shard_map/split | solution.py:127
Sparse Core Ops, SparseCore 0:
  18.8 22.8 all-gather.7
  43.2 22.5 all-gather.3
  67.4 22.5 all-gather.5
